TPU v7x, 256 devices: a whole 4x4x8 slice. The times are simulated.
256 devices in a mesh: gx: 32 (over x, y, core), gy: 8 (over z).
Axes of the slice: x: 4, y: 4, z: 8, core: 2. Of those that a mesh axis runs over, the one named last changes fastest.
Arguments:
- orbitals: float32 [64, 128, 64, 128], P(None, 'gx', 'gy'), may hold values from -60 to 60, as said below
- potential: float32 [128, 64, 128], P('gx', 'gy'), may hold values from 0.2 to 2
Outputs:
- basis: float32 [64, 128, 64, 128], P(None, 'gx', 'gy')
- factor: float32 [64, 64], replicated
Inputs may be any that keep to these rules, and one draw needn't show every extreme that they name: `orbitals`: Real-valued entries.
All inputs are finite; a program needn't handle non-finite values.
Results may differ from a plain program's by a relative error of at most 0.00011.
Values sent between devices are 32-bit elements; how exact they have to be, the bound alone decides.
No kernel may reach another device: no remote copies, remote signals or barrier semaphores. Data moves between devices by JAX's collectives and lax.ppermute only.
A program may use at most 64 MiB of HBM per device.

v0:
```python
import jax
import jax.numpy as jnp
from jax import lax
from jax.sharding import PartitionSpec as P


def extended(cells, sides, width):
    for axis, dim in sides:
        count = lax.axis_size(axis)
        head = lax.slice_in_dim(cells, 0, width, axis=dim)
        tail = lax.slice_in_dim(cells, cells.shape[dim] - width, cells.shape[dim], axis=dim)
        cells = jnp.concatenate(
            [
                lax.ppermute(tail, axis, [(i, (i + 1) % count) for i in range(count)]),
                cells,
                lax.ppermute(head, axis, [((i + 1) % count, i) for i in range(count)]),
            ],
            axis=dim,
        )
    return cells


def apply_ham(padded, pot):
    core = padded[:, 2:-2, 2:-2]
    total = -7.5 * core
    total = total + 4.0 / 3.0 * (padded[:, 3:-1, 2:-2] + padded[:, 1:-3, 2:-2])
    total = total - 1.0 / 12.0 * (padded[:, 4:, 2:-2] + padded[:, :-4, 2:-2])
    total = total + 4.0 / 3.0 * (padded[:, 2:-2, 3:-1] + padded[:, 2:-2, 1:-3])
    total = total - 1.0 / 12.0 * (padded[:, 2:-2, 4:] + padded[:, 2:-2, :-4])
    total = total + 4.0 / 3.0 * (jnp.roll(core, 1, 3) + jnp.roll(core, -1, 3))
    total = total - 1.0 / 12.0 * (jnp.roll(core, 2, 3) + jnp.roll(core, -2, 3))
    return -0.5 * total + pot[None] * core


def with_faces(field):
    return extended(field, (("gx", 1), ("gy", 2)), 2)


def upper_factor(gram):
    order = gram.shape[0]
    index = jnp.arange(order)

    def column_step(col, lower):
        row_now = lax.dynamic_slice_in_dim(lower, col, 1, 0)[0]
        target = lax.dynamic_slice_in_dim(gram, col, 1, 1)[:, 0]
        column = target - jnp.dot(
            lower, row_now, precision=lax.Precision.HIGHEST, preferred_element_type=jnp.float32
        )
        pivot = jnp.sqrt(jnp.sum(jnp.where(index == col, column, 0.0)))
        values = jnp.where(index == col, pivot, column / pivot)
        values = jnp.where(index >= col, values, 0.0)
        return jnp.where(index[None, :] == col, values[:, None], lower)

    lower = lax.fori_loop(0, order, column_step, jnp.zeros_like(gram))
    return lower.T


def upper_inverse(upper):
    order = upper.shape[0]
    index = jnp.arange(order)

    def row_step(step, inverse):
        row = order - 1 - step
        upper_row = lax.dynamic_slice_in_dim(upper, row, 1, 0)[0]
        pivot = jnp.sum(jnp.where(index == row, upper_row, 0.0))
        rest = jnp.dot(
            upper_row, inverse, precision=lax.Precision.HIGHEST, preferred_element_type=jnp.float32
        )
        unit = jnp.where(index == row, 1.0, 0.0).astype(jnp.float32)
        new_row = (unit - rest) / pivot
        return jnp.where(index[:, None] == row, new_row[None, :], inverse)

    return lax.fori_loop(0, order, row_step, jnp.zeros_like(upper))


def shards(orbitals, potential):
    first = (apply_ham(with_faces(orbitals), potential) - 5.5 * orbitals) / 4.5
    applied = apply_ham(with_faces(first), potential)
    filtered = 2.0 * (applied - 5.5 * first) / 4.5 - orbitals
    width = filtered.shape[0]
    flat = filtered.reshape(width, -1)
    cells = flat.shape[1] * lax.axis_size("gx") * lax.axis_size("gy")
    local_gram = (
        jnp.dot(flat, flat.T, precision=lax.Precision.HIGHEST, preferred_element_type=jnp.float32)
        / cells
    )
    factor = upper_factor(lax.psum(local_gram, ("gx", "gy")))
    inverse = upper_inverse(factor)
    solved = jnp.dot(
        inverse.T, flat, precision=lax.Precision.HIGHEST, preferred_element_type=jnp.float32
    )
    basis = (solved * jnp.sqrt(jnp.float32(cells))).reshape(filtered.shape)
    return (basis, factor)


def solution(mesh):
    return jax.shard_map(
        shards,
        mesh=mesh,
        in_specs=(P(None, "gx", "gy", None), P("gx", "gy", None)),
        out_specs=(P(None, "gx", "gy", None), P()),
        check_vma=False,
    )
```

profile of v0, /device:TPU:1, one launch (start us, length us, event | category | flops | bytes accessed | tf_op | source)
XLA Modules:
  0.0 353.4 jit_solution(158170441676691293)
XLA Ops:
  0.6 2.4 fusion.60
  3.0 3.2 collective-permute-start
  8.3 4.5 %collective-permute-done = f32[64,2,8,128]{3,2,1,0:T(8,128)S(1)} collective-permute-done((f32[64,2,8,128]{3,2,1,0:T(8,128)}, f32[64,2,8,128]{3,2,1,0:T(8,128)S(1)}, u32[]{:S(2)}, u32[]{:S(2)}) %collective-permute-start) | collective-permute-done | bytes 524320 | tf_op jit(solution)/shard_map/ppermute | solution.py:16
  13.7 5.7 %collective-permute-start.2 = (f32[64,8,2,128]{3,1,2,0:T(8,128)S(1)}, f32[64,8,2,128]{3,1,2,0:T(8,128)S(1)}, u32[]{:S(2)}, u32[]{:S(2)}) collective-permute-start(f32[64,8,2,128]{3,1,2,0:T(8,128)S(1)} %get-tuple-element.266), channel_id=1, source_target_pairs={{1,0},{2,1},{3,2},{4,3},{5,4},{6,5},{7,6},{0,7},{9,8},{10,9},{11,1... | collective-permute-start | bytes 1572872 | tf_op jit(solution)/shard_map/ppermute | solution.py:16
  20.6 4.8 %collective-permute-done.2 = f32[64,8,2,128]{3,1,2,0:T(8,128)S(1)} collective-permute-done((f32[64,8,2,128]{3,1,2,0:T(8,128)S(1)}, f32[64,8,2,128]{3,1,2,0:T(8,128)S(1)}, u32[]{:S(2)}, u32[]{:S(2)}) %collective-permute-start.2) | collective-permute-done | bytes 524320 | tf_op jit(solution)/shard_map/ppermute | solution.py:16
  25.4 3.1 collective-permute-done.3
  28.6 7.3 %broadcast_multiply_fusion = (f32[64,4,8,128]{3,1,2,0:T(4,128)S(1)}, f32[64,4,8,128]{3,1,2,0:T(4,128)S(1)}) fusion(f32[64,4,8,128]{3,1,2,0:T(4,128)S(1)} %copy.55, f32[4,8,128]{2,0,1:T(4,128)S(1)} %copy.71, f32[64,4,8,2]{3,1,2,0:T(4,128)S(1)} %get-tuple-element.285, f32[64,4,8,126]{3,1,2,0:T(4,128)S(1)} %get-tuple-element.287, ...), kind=kLoop, calls=%fused_computation.105 | loop fusion | flops 11796480 | bytes 9453568 | tf_op jit(solution)/shard_map/div | solution.py:77
  36.4 9.8 %collective-permute-start.4 = (f32[64,2,8,128]{3,2,1,0:T(8,128)S(1)}, f32[64,2,8,128]{3,2,1,0:T(8,128)S(1)}, u32[]{:S(2)}, u32[]{:S(2)}) collective-permute-start(f32[64,2,8,128]{3,2,1,0:T(8,128)S(1)} %copy.74), channel_id=1, source_target_pairs={{8,0},{16,8},{24,16},{32,24},{40,32},{48,40},{56,48},{64,56},{72,6... | collective-permute-start | bytes 1572872 | tf_op jit(solution)/shard_map/ppermute | solution.py:16
  47.7 3.3 collective-permute-done.4
  51.3 1.3 collective-permute-done.5
  53.3 1.5 collective-permute-start.7
  56.0 5.3 %collective-permute-done.6 = f32[64,8,2,128]{3,1,2,0:T(8,128)S(1)} collective-permute-done((f32[64,8,2,128]{3,1,2,0:T(8,128)S(1)}, f32[64,8,2,128]{3,1,2,0:T(8,128)S(1)}, u32[]{:S(2)}, u32[]{:S(2)}) %collective-permute-start.6) | collective-permute-done | bytes 524320 | tf_op jit(solution)/shard_map/ppermute | solution.py:16
  61.3 1.3 collective-permute-done.7
  62.6 7.5 %multiply_subtract_fusion = f32[64,4,8,128]{3,1,2,0:T(4,128)S(1)} fusion(f32[64,4,8,128]{3,1,2,0:T(4,128)S(1)} %get-tuple-element.261, f32[64,4,8,2]{3,1,2,0:T(4,128)S(1)} %get-tuple-element.275, f32[64,4,8,126]{3,1,2,0:T(4,128)S(1)} %get-tuple-element.277, f32[64,4,8,126]{3,1,2,0:T(4,128)S(1)} %get-tuple-element.276, ...), kind=kLoop, calls=%fused_computation.97 | loop fusion | flops 12058624 | bytes 10502144 | tf_op jit(solution)/shard_map/sub | solution.py:79
  70.1 2.1 fusion.17
  72.2 81.9 %psum.7 = f32[64,64]{1,0:T(8,128)S(1)} all-reduce(f32[64,64]{1,0:T(8,128)S(1)} %fusion.17), channel_id=1, replica_groups=mesh['gx'=32,'gy'=8] {'gx','gy'}, use_global_device_ids=true, to_apply=%region_0.1 | all-reduce | flops 4096 | bytes 32768 | tf_op jit(solution)/shard_map/psum | solution.py:87
  154.2 101.3 %while.32 = (s32[]{:T(128)}, f32[64,64]{1,0:T(8,128)S(1)}, f32[64,64]{0,1:T(8,128)S(1)}, s32[]{:T(128)}, s32[]{:T(128)}) while((s32[]{:T(128)}, f32[64,64]{1,0:T(8,128)S(1)}, f32[64,64]{0,1:T(8,128)S(1)}, s32[]{:T(128)}, s32[]{:T(128)}) %tuple.94), condition=%wide.region_3.4_spmd.clone.clone, body=%wide.region_1.3_spmd.clone.clone.sunk | while | flops 62082 | bytes 102112 | solution.py:54
  255.6 95.1 %while.31 = (s32[]{:T(128)}, f32[64,64]{1,0:T(8,128)S(1)}, f32[64,64]{1,0:T(8,128)S(1)}, s32[]{:T(128)}, s32[]{:T(128)}, /*index=5*/s32[]{:T(128)}, s32[]{:T(128)}) while((s32[]{:T(128)}, f32[64,64]{1,0:T(8,128)S(1)}, f32[64,64]{1,0:T(8,128)S(1)}, s32[]{:T(128)}, s32[]{:T(128)}, /*index=5*/s32[]{:T(128)}, s32[]{:T(128)}) %tuple.100), condition=%wide.region_6.7_spmd.clone, body=%wide.region_4.6_spmd.clone.sunk | while | flops 61958 | bytes 67106 | solution.py:73
  256.2 0.8 fusion.75
  257.7 0.8 fusion.75
  259.1 0.8 fusion.75
  262.1 0.8 fusion.75
  263.6 0.8 fusion.75
  265.1 0.8 fusion.75
  266.6 0.8 fusion.75
  268.1 0.8 fusion.75
  271.0 0.8 fusion.75
  272.5 0.8 fusion.75
  274.0 0.8 fusion.75
  275.5 0.8 fusion.75
  277.0 0.8 fusion.75
  278.5 0.8 fusion.75
  279.9 0.8 fusion.75
  281.4 0.8 fusion.75
  282.9 0.8 fusion.75
  284.4 0.8 fusion.75
  285.9 0.8 fusion.75
  287.4 0.8 fusion.75
  290.3 0.8 fusion.75
  291.8 0.8 fusion.75
  293.3 0.8 fusion.75
  294.8 0.8 fusion.75
  296.3 0.8 fusion.75
  299.2 0.8 fusion.75
  300.7 0.8 fusion.75
  302.2 0.8 fusion.75
  303.7 0.8 fusion.75
  305.2 0.8 fusion.75
  306.7 0.8 fusion.75
  308.2 0.8 fusion.75
  309.6 0.8 fusion.75
  311.1 0.8 fusion.75
  312.6 0.8 fusion.75
  314.1 0.8 fusion.75
  315.6 0.8 fusion.75
  318.6 0.8 fusion.75
  320.0 0.8 fusion.75
  321.5 0.8 fusion.75
  323.0 0.8 fusion.75
  324.5 0.8 fusion.75
  327.5 0.8 fusion.75
  329.0 0.8 fusion.75
  350.6 1.6 fusion.16
  352.2 1.2 copy.89
  (569 shorter events, 124.5 us)
Async XLA Ops:
  0.6 5.6 %copy-start = (f32[64,4,8,128]{3,2,1,0:T(8,128)S(1)}, f32[64,4,8,128]{3,2,1,0:T(8,128)}, u32[]{:S(2)}) copy-start(f32[64,4,8,128]{3,2,1,0:T(8,128)} %param.6) | copy-start | bytes 3145732
  3.0 9.8 %collective-permute-start = (f32[64,2,8,128]{3,2,1,0:T(8,128)}, f32[64,2,8,128]{3,2,1,0:T(8,128)S(1)}, u32[]{:S(2)}, u32[]{:S(2)}) collective-permute-start(f32[64,2,8,128]{3,2,1,0:T(8,128)} %get-tuple-element.279), channel_id=1, source_target_pairs={{8,0},{16,8},{24,16},{32,24},{40,32},{48,40},{56,48},{64,56},{72,6... | collective-permute-start | bytes 1572872 | tf_op jit(solution)/shard_map/ppermute | solution.py:16
  6.2 0.7 copy-start.1
  6.2 6.8 %collective-permute-start.1 = (f32[64,2,8,128]{3,2,1,0:T(8,128)}, f32[64,2,8,128]{3,2,1,0:T(8,128)S(1)}, u32[]{:S(2)}, u32[]{:S(2)}) collective-permute-start(f32[64,2,8,128]{3,2,1,0:T(8,128)} %get-tuple-element.278), channel_id=1, source_target_pairs={{0,8},{8,16},{16,24},{24,32},{32,40},{40,48},{48,56},{56,64},{64,7... | collective-permute-start | bytes 1572872 | tf_op jit(solution)/shard_map/ppermute | solution.py:14
  13.7 11.8 %collective-permute-start.2 = (f32[64,8,2,128]{3,1,2,0:T(8,128)S(1)}, f32[64,8,2,128]{3,1,2,0:T(8,128)S(1)}, u32[]{:S(2)}, u32[]{:S(2)}) collective-permute-start(f32[64,8,2,128]{3,1,2,0:T(8,128)S(1)} %get-tuple-element.266), channel_id=1, source_target_pairs={{1,0},{2,1},{3,2},{4,3},{5,4},{6,5},{7,6},{0,7},{9,8},{10,9},{11,1... | collective-permute-start | bytes 1572872 | tf_op jit(solution)/shard_map/ppermute | solution.py:16
  19.3 9.2 %collective-permute-start.3 = (f32[64,8,2,128]{3,1,2,0:T(8,128)S(1)}, f32[64,8,2,128]{3,1,2,0:T(8,128)S(1)}, u32[]{:S(2)}, u32[]{:S(2)}) collective-permute-start(f32[64,8,2,128]{3,1,2,0:T(8,128)S(1)} %get-tuple-element.267), channel_id=1, source_target_pairs={{0,1},{1,2},{2,3},{3,4},{4,5},{5,6},{6,7},{7,0},{8,9},{9,10},{10,1... | collective-permute-start | bytes 1572872 | tf_op jit(solution)/shard_map/ppermute | solution.py:14
  36.4 14.6 %collective-permute-start.4 = (f32[64,2,8,128]{3,2,1,0:T(8,128)S(1)}, f32[64,2,8,128]{3,2,1,0:T(8,128)S(1)}, u32[]{:S(2)}, u32[]{:S(2)}) collective-permute-start(f32[64,2,8,128]{3,2,1,0:T(8,128)S(1)} %copy.74), channel_id=1, source_target_pairs={{8,0},{16,8},{24,16},{32,24},{40,32},{48,40},{56,48},{64,56},{72,6... | collective-permute-start | bytes 1572872 | tf_op jit(solution)/shard_map/ppermute | solution.py:16
  46.2 6.4 %collective-permute-start.5 = (f32[64,2,8,128]{3,2,1,0:T(8,128)S(1)}, f32[64,2,8,128]{3,2,1,0:T(8,128)S(1)}, u32[]{:S(2)}, u32[]{:S(2)}) collective-permute-start(f32[64,2,8,128]{3,2,1,0:T(8,128)S(1)} %copy.76), channel_id=1, source_target_pairs={{0,8},{8,16},{16,24},{24,32},{32,40},{40,48},{48,56},{56,64},{64,7... | collective-permute-start | bytes 1572872 | tf_op jit(solution)/shard_map/ppermute | solution.py:14
  53.2 8.1 %collective-permute-start.6 = (f32[64,8,2,128]{3,1,2,0:T(8,128)S(1)}, f32[64,8,2,128]{3,1,2,0:T(8,128)S(1)}, u32[]{:S(2)}, u32[]{:S(2)}) collective-permute-start(f32[64,8,2,128]{3,1,2,0:T(8,128)S(1)} %get-tuple-element.264), channel_id=1, source_target_pairs={{1,0},{2,1},{3,2},{4,3},{5,4},{6,5},{7,6},{0,7},{9,8},{10,9},{11,1... | collective-permute-start | bytes 1572872 | tf_op jit(solution)/shard_map/ppermute | solution.py:16
  53.3 9.3 %collective-permute-start.7 = (f32[64,8,2,128]{3,1,2,0:T(8,128)S(1)}, f32[64,8,2,128]{3,1,2,0:T(8,128)S(1)}, u32[]{:S(2)}, u32[]{:S(2)}) collective-permute-start(f32[64,8,2,128]{3,1,2,0:T(8,128)S(1)} %get-tuple-element.265), channel_id=1, source_target_pairs={{0,1},{1,2},{2,3},{3,4},{4,5},{5,6},{6,7},{7,0},{8,9},{9,10},{10,1... | collective-permute-start | bytes 1572872 | tf_op jit(solution)/shard_map/ppermute | solution.py:14
  350.6 1.6 copy-start.2
where the time goes:
time: 355 us; the launch traced here: 353 us
  matrix products  103 us (29%)
  blocking collectives  81.9 us (23%)
  other arithmetic  66.1 us (19%)
  loops' own time  46 us (13%)
  waiting for transfers between devices  23.6 us (7%)
  starting transfers between devices  20.4 us (6%)
  local copies, waits for them, and re-layouts  11.1 us (3%)
    psum x1, blocking collectives, shards(): factor = upper_factor(lax.psum(local_gram, ('gx', 'gy')))  81.9 us
    dot_general x64, matrix products, row_step(): jnp.dot(upper_row, inverse, precision=lax.Precision.HIGHEST, preferred_el...  50.1 us
    dot_general x64, matrix products, column_step(): jnp.dot(lower, row_now, precision=lax.Precision.HIGHEST, preferred_elemen...  49.5 us
    another operation x1, loops' own time, upper_factor(): lower = lax.fori_loop(0, order, column_step, jnp.zeros_like(gram))  45.6 us
    reduce_sum x64, other arithmetic, row_step(): pivot = jnp.sum(jnp.where(index == row, upper_row, 0.0))  39.3 us
    ppermute x4, starting transfers between devices, extended(): lax.ppermute(head, axis, [((i + 1) % count, i) for i in range(count)])  18.7 us
    ppermute x4, waiting for transfers between devices, extended(): lax.ppermute(head, axis, [((i + 1) % count, i) for i in range(count)])  17.9 us
    sub x1, other arithmetic, shards(): filtered = 2.0 * (applied - 5.5 * first) / 4.5 - orbitals  7.45 us
  transfers between devices with their start and end apart: 8, of which 7 were waited for; matrix products, arithmetic and copies ran while one was open for 2% of the time, Pallas kernels for 0%

commit v1 on v0

--- a/solution.py
+++ b/solution.py
@@ -84,7 +84,7 @@
         jnp.dot(flat, flat.T, precision=lax.Precision.HIGHEST, preferred_element_type=jnp.float32)
         / cells
     )
-    factor = upper_factor(lax.psum(local_gram, ("gx", "gy")))
+    factor = upper_factor(lax.psum(lax.psum(local_gram, "gy"), "gx"))
     inverse = upper_inverse(factor)
     solved = jnp.dot(
         inverse.T, flat, precision=lax.Precision.HIGHEST, preferred_element_type=jnp.float32

time: 355 us -> 430 us (1.21)
  blocking collectives: 81.9 us -> 155 us
    psum x1 -> x2, blocking collectives: 81.9 us -> 155 us  [shards(): factor = upper_factor(lax.psum(lax.psum(local_gram, 'gy'), 'gx'))]
  transfers between devices with their start and end apart: 8 -> 8, of which waited for: 7 -> 7; matrix products, arithmetic and copies ran while one was open for 2% -> 1% of each run, Pallas kernels for 0% -> 0%
where the time goes in v1:
time: 430 us; the launch traced here: 427 us
  blocking collectives  155 us (36%)
  matrix products  103 us (24%)
  other arithmetic  66.1 us (15%)
  loops' own time  46 us (11%)
  waiting for transfers between devices  23.6 us (5%)
  starting transfers between devices  20.4 us (5%)
  local copies, waits for them, and re-layouts  11.1 us (3%)
    psum x2, blocking collectives, shards(): factor = upper_factor(lax.psum(lax.psum(local_gram, 'gy'), 'gx'))  155 us
    dot_general x64, matrix products, row_step(): jnp.dot(upper_row, inverse, precision=lax.Precision.HIGHEST, preferred_el...  50.1 us
    dot_general x64, matrix products, column_step(): jnp.dot(lower, row_now, precision=lax.Precision.HIGHEST, preferred_elemen...  49.5 us
    another operation x1, loops' own time, upper_factor(): lower = lax.fori_loop(0, order, column_step, jnp.zeros_like(gram))  45.6 us
    reduce_sum x64, other arithmetic, row_step(): pivot = jnp.sum(jnp.where(index == row, upper_row, 0.0))  39.3 us
    ppermute x4, starting transfers between devices, extended(): lax.ppermute(head, axis, [((i + 1) % count, i) for i in range(count)])  18.7 us
    ppermute x4, waiting for transfers between devices, extended(): lax.ppermute(head, axis, [((i + 1) % count, i) for i in range(count)])  17.9 us
  transfers between devices with their start and end apart: 8, of which 7 were waited for; matrix products, arithmetic and copies ran while one was open for 1% of the time, Pallas kernels for 0%

profile of v1, /device:TPU:1, one launch (start us, length us, event | category | flops | bytes accessed | tf_op | source)
XLA Modules:
  0.0 426.7 jit_solution(15361000754226975613)
XLA Ops:
  0.6 2.3 fusion.60
  3.0 3.2 collective-permute-start
  8.3 4.5 %collective-permute-done = f32[64,2,8,128]{3,2,1,0:T(8,128)S(1)} collective-permute-done((f32[64,2,8,128]{3,2,1,0:T(8,128)}, f32[64,2,8,128]{3,2,1,0:T(8,128)S(1)}, u32[]{:S(2)}, u32[]{:S(2)}) %collective-permute-start) | collective-permute-done | bytes 524320 | tf_op jit(solution)/shard_map/ppermute | solution.py:16
  13.6 5.7 %collective-permute-start.2 = (f32[64,8,2,128]{3,1,2,0:T(8,128)S(1)}, f32[64,8,2,128]{3,1,2,0:T(8,128)S(1)}, u32[]{:S(2)}, u32[]{:S(2)}) collective-permute-start(f32[64,8,2,128]{3,1,2,0:T(8,128)S(1)} %get-tuple-element.266), channel_id=1, source_target_pairs={{1,0},{2,1},{3,2},{4,3},{5,4},{6,5},{7,6},{0,7},{9,8},{10,9},{11,1... | collective-permute-start | bytes 1572872 | tf_op jit(solution)/shard_map/ppermute | solution.py:16
  20.6 4.8 %collective-permute-done.2 = f32[64,8,2,128]{3,1,2,0:T(8,128)S(1)} collective-permute-done((f32[64,8,2,128]{3,1,2,0:T(8,128)S(1)}, f32[64,8,2,128]{3,1,2,0:T(8,128)S(1)}, u32[]{:S(2)}, u32[]{:S(2)}) %collective-permute-start.2) | collective-permute-done | bytes 524320 | tf_op jit(solution)/shard_map/ppermute | solution.py:16
  25.4 3.1 collective-permute-done.3
  28.5 7.3 %broadcast_multiply_fusion = (f32[64,4,8,128]{3,1,2,0:T(4,128)S(1)}, f32[64,4,8,128]{3,1,2,0:T(4,128)S(1)}) fusion(f32[64,4,8,128]{3,1,2,0:T(4,128)S(1)} %copy.55, f32[4,8,128]{2,0,1:T(4,128)S(1)} %copy.71, f32[64,4,8,2]{3,1,2,0:T(4,128)S(1)} %get-tuple-element.285, f32[64,4,8,126]{3,1,2,0:T(4,128)S(1)} %get-tuple-element.287, ...), kind=kLoop, calls=%fused_computation.105 | loop fusion | flops 11796480 | bytes 9453568 | tf_op jit(solution)/shard_map/div | solution.py:77
  36.4 9.8 %collective-permute-start.4 = (f32[64,2,8,128]{3,2,1,0:T(8,128)S(1)}, f32[64,2,8,128]{3,2,1,0:T(8,128)S(1)}, u32[]{:S(2)}, u32[]{:S(2)}) collective-permute-start(f32[64,2,8,128]{3,2,1,0:T(8,128)S(1)} %copy.74), channel_id=1, source_target_pairs={{8,0},{16,8},{24,16},{32,24},{40,32},{48,40},{56,48},{64,56},{72,6... | collective-permute-start | bytes 1572872 | tf_op jit(solution)/shard_map/ppermute | solution.py:16
  47.7 3.3 collective-permute-done.4
  51.3 1.3 collective-permute-done.5
  53.3 1.5 collective-permute-start.7
  56.0 5.3 %collective-permute-done.6 = f32[64,8,2,128]{3,1,2,0:T(8,128)S(1)} collective-permute-done((f32[64,8,2,128]{3,1,2,0:T(8,128)S(1)}, f32[64,8,2,128]{3,1,2,0:T(8,128)S(1)}, u32[]{:S(2)}, u32[]{:S(2)}) %collective-permute-start.6) | collective-permute-done | bytes 524320 | tf_op jit(solution)/shard_map/ppermute | solution.py:16
  61.3 1.3 collective-permute-done.7
  62.6 7.5 %multiply_subtract_fusion = f32[64,4,8,128]{3,1,2,0:T(4,128)S(1)} fusion(f32[64,4,8,128]{3,1,2,0:T(4,128)S(1)} %get-tuple-element.261, f32[64,4,8,2]{3,1,2,0:T(4,128)S(1)} %get-tuple-element.275, f32[64,4,8,126]{3,1,2,0:T(4,128)S(1)} %get-tuple-element.277, f32[64,4,8,126]{3,1,2,0:T(4,128)S(1)} %get-tuple-element.276, ...), kind=kLoop, calls=%fused_computation.97 | loop fusion | flops 12058624 | bytes 10502144 | tf_op jit(solution)/shard_map/sub | solution.py:79
  70.1 2.1 fusion.17
  72.2 20.1 %psum.14 = f32[64,64]{1,0:T(8,128)S(1)} all-reduce(f32[64,64]{1,0:T(8,128)S(1)} %fusion.17), channel_id=1, replica_groups=mesh['gx'=32,'gy'=8] {'gy'}, use_global_device_ids=true, to_apply=%region_0.1 | all-reduce | flops 4096 | bytes 32768 | tf_op jit(solution)/shard_map/psum | solution.py:87
  92.4 135.0 %psum.15 = f32[64,64]{1,0:T(8,128)S(1)} all-reduce(f32[64,64]{1,0:T(8,128)S(1)} %psum.14), channel_id=1, replica_groups=mesh['gx'=32,'gy'=8] {'gx'}, use_global_device_ids=true, to_apply=%region_1.2 | all-reduce | flops 4096 | bytes 32768 | tf_op jit(solution)/shard_map/psum | solution.py:87
  227.4 101.3 %while.32 = (s32[]{:T(128)}, f32[64,64]{1,0:T(8,128)S(1)}, f32[64,64]{0,1:T(8,128)S(1)}, s32[]{:T(128)}, s32[]{:T(128)}) while((s32[]{:T(128)}, f32[64,64]{1,0:T(8,128)S(1)}, f32[64,64]{0,1:T(8,128)S(1)}, s32[]{:T(128)}, s32[]{:T(128)}) %tuple.94), condition=%wide.region_4.5_spmd.clone.clone, body=%wide.region_2.4_spmd.clone.clone.sunk | while | flops 62082 | bytes 102112 | solution.py:54
  328.8 95.1 %while.31 = (s32[]{:T(128)}, f32[64,64]{1,0:T(8,128)S(1)}, f32[64,64]{1,0:T(8,128)S(1)}, s32[]{:T(128)}, s32[]{:T(128)}, /*index=5*/s32[]{:T(128)}, s32[]{:T(128)}) while((s32[]{:T(128)}, f32[64,64]{1,0:T(8,128)S(1)}, f32[64,64]{1,0:T(8,128)S(1)}, s32[]{:T(128)}, s32[]{:T(128)}, /*index=5*/s32[]{:T(128)}, s32[]{:T(128)}) %tuple.100), condition=%wide.region_7.8_spmd.clone, body=%wide.region_5.7_spmd.clone.sunk | while | flops 61958 | bytes 67106 | solution.py:73
  329.4 0.8 fusion.75
  330.9 0.8 fusion.75
  333.9 0.8 fusion.75
  335.4 0.8 fusion.75
  336.9 0.8 fusion.75
  338.3 0.8 fusion.75
  339.8 0.8 fusion.75
  341.3 0.8 fusion.75
  342.8 0.8 fusion.75
  344.3 0.8 fusion.75
  345.8 0.8 fusion.75
  347.3 0.8 fusion.75
  348.7 0.8 fusion.75
  350.2 0.8 fusion.75
  353.2 0.8 fusion.75
  354.7 0.8 fusion.75
  356.2 0.8 fusion.75
  357.7 0.8 fusion.75
  359.1 0.8 fusion.75
  362.1 0.8 fusion.75
  363.6 0.8 fusion.75
  365.1 0.8 fusion.75
  366.6 0.8 fusion.75
  368.0 0.8 fusion.75
  369.5 0.8 fusion.75
  371.0 0.8 fusion.75
  372.5 0.8 fusion.75
  374.0 0.8 fusion.75
  375.5 0.8 fusion.75
  377.0 0.8 fusion.75
  378.4 0.8 fusion.75
  381.4 0.8 fusion.75
  382.9 0.8 fusion.75
  384.4 0.8 fusion.75
  385.9 0.8 fusion.75
  387.4 0.8 fusion.75
  390.3 0.8 fusion.75
  391.8 0.8 fusion.75
  393.3 0.8 fusion.75
  394.8 0.8 fusion.75
  396.3 0.8 fusion.75
  397.8 0.8 fusion.75
  399.2 0.8 fusion.75
  423.9 1.6 fusion.16
  425.5 1.2 copy.89
  (570 shorter events, 125.3 us)
Async XLA Ops:
  0.6 5.6 %copy-start = (f32[64,4,8,128]{3,2,1,0:T(8,128)S(1)}, f32[64,4,8,128]{3,2,1,0:T(8,128)}, u32[]{:S(2)}) copy-start(f32[64,4,8,128]{3,2,1,0:T(8,128)} %param.6) | copy-start | bytes 3145732
  3.0 9.8 %collective-permute-start = (f32[64,2,8,128]{3,2,1,0:T(8,128)}, f32[64,2,8,128]{3,2,1,0:T(8,128)S(1)}, u32[]{:S(2)}, u32[]{:S(2)}) collective-permute-start(f32[64,2,8,128]{3,2,1,0:T(8,128)} %get-tuple-element.279), channel_id=1, source_target_pairs={{8,0},{16,8},{24,16},{32,24},{40,32},{48,40},{56,48},{64,56},{72,6... | collective-permute-start | bytes 1572872 | tf_op jit(solution)/shard_map/ppermute | solution.py:16
  6.2 0.7 copy-start.1
  6.2 6.8 %collective-permute-start.1 = (f32[64,2,8,128]{3,2,1,0:T(8,128)}, f32[64,2,8,128]{3,2,1,0:T(8,128)S(1)}, u32[]{:S(2)}, u32[]{:S(2)}) collective-permute-start(f32[64,2,8,128]{3,2,1,0:T(8,128)} %get-tuple-element.278), channel_id=1, source_target_pairs={{0,8},{8,16},{16,24},{24,32},{32,40},{40,48},{48,56},{56,64},{64,7... | collective-permute-start | bytes 1572872 | tf_op jit(solution)/shard_map/ppermute | solution.py:14
  13.6 11.8 %collective-permute-start.2 = (f32[64,8,2,128]{3,1,2,0:T(8,128)S(1)}, f32[64,8,2,128]{3,1,2,0:T(8,128)S(1)}, u32[]{:S(2)}, u32[]{:S(2)}) collective-permute-start(f32[64,8,2,128]{3,1,2,0:T(8,128)S(1)} %get-tuple-element.266), channel_id=1, source_target_pairs={{1,0},{2,1},{3,2},{4,3},{5,4},{6,5},{7,6},{0,7},{9,8},{10,9},{11,1... | collective-permute-start | bytes 1572872 | tf_op jit(solution)/shard_map/ppermute | solution.py:16
  19.3 9.2 %collective-permute-start.3 = (f32[64,8,2,128]{3,1,2,0:T(8,128)S(1)}, f32[64,8,2,128]{3,1,2,0:T(8,128)S(1)}, u32[]{:S(2)}, u32[]{:S(2)}) collective-permute-start(f32[64,8,2,128]{3,1,2,0:T(8,128)S(1)} %get-tuple-element.267), channel_id=1, source_target_pairs={{0,1},{1,2},{2,3},{3,4},{4,5},{5,6},{6,7},{7,0},{8,9},{9,10},{10,1... | collective-permute-start | bytes 1572872 | tf_op jit(solution)/shard_map/ppermute | solution.py:14
  36.4 14.6 %collective-permute-start.4 = (f32[64,2,8,128]{3,2,1,0:T(8,128)S(1)}, f32[64,2,8,128]{3,2,1,0:T(8,128)S(1)}, u32[]{:S(2)}, u32[]{:S(2)}) collective-permute-start(f32[64,2,8,128]{3,2,1,0:T(8,128)S(1)} %copy.74), channel_id=1, source_target_pairs={{8,0},{16,8},{24,16},{32,24},{40,32},{48,40},{56,48},{64,56},{72,6... | collective-permute-start | bytes 1572872 | tf_op jit(solution)/shard_map/ppermute | solution.py:16
  46.1 6.4 %collective-permute-start.5 = (f32[64,2,8,128]{3,2,1,0:T(8,128)S(1)}, f32[64,2,8,128]{3,2,1,0:T(8,128)S(1)}, u32[]{:S(2)}, u32[]{:S(2)}) collective-permute-start(f32[64,2,8,128]{3,2,1,0:T(8,128)S(1)} %copy.76), channel_id=1, source_target_pairs={{0,8},{8,16},{16,24},{24,32},{32,40},{40,48},{48,56},{56,64},{64,7... | collective-permute-start | bytes 1572872 | tf_op jit(solution)/shard_map/ppermute | solution.py:14
  53.2 8.1 %collective-permute-start.6 = (f32[64,8,2,128]{3,1,2,0:T(8,128)S(1)}, f32[64,8,2,128]{3,1,2,0:T(8,128)S(1)}, u32[]{:S(2)}, u32[]{:S(2)}) collective-permute-start(f32[64,8,2,128]{3,1,2,0:T(8,128)S(1)} %get-tuple-element.264), channel_id=1, source_target_pairs={{1,0},{2,1},{3,2},{4,3},{5,4},{6,5},{7,6},{0,7},{9,8},{10,9},{11,1... | collective-permute-start | bytes 1572872 | tf_op jit(solution)/shard_map/ppermute | solution.py:16
  53.3 9.3 %collective-permute-start.7 = (f32[64,8,2,128]{3,1,2,0:T(8,128)S(1)}, f32[64,8,2,128]{3,1,2,0:T(8,128)S(1)}, u32[]{:S(2)}, u32[]{:S(2)}) collective-permute-start(f32[64,8,2,128]{3,1,2,0:T(8,128)S(1)} %get-tuple-element.265), channel_id=1, source_target_pairs={{0,1},{1,2},{2,3},{3,4},{4,5},{5,6},{6,7},{7,0},{8,9},{9,10},{10,1... | collective-permute-start | bytes 1572872 | tf_op jit(solution)/shard_map/ppermute | solution.py:14
  423.9 1.6 copy-start.2
